TPU v7x, 256 devices: a whole 4x4x8 slice. The times are simulated.
256 devices in a mesh: dp: 16 (over y, x), section: 2 (over core), tensor: 8 (over z).
Axes of the slice: x: 4, y: 4, z: 8, core: 2. Of those that a mesh axis runs over, the one named last changes fastest.
Arguments:
- tokens: bfloat16 [2048, 16384], P('dp'), may hold values from -9 to 9
- order: int32 [2048], replicated, may hold values from 0 to 2047, as said below
- segments: int32 [2048], replicated, may hold values from 0 to 1, as said below
- gain: float32 [2, 16384], P('section', 'dp'), may hold values from 0.1 to 1.9
- w_query: bfloat16 [2, 16384, 8192], P('section', 'dp', 'tensor'), may hold values from -0.046875 to 0.046875
- key_value_weight: bfloat16 [2, 16384, 8, 256], P('section', 'dp', 'tensor'), may hold values from -0.046875 to 0.046875
- w_out: bfloat16 [2, 8192, 16384], P('section', 'tensor', 'dp'), may hold values from -0.0625 to 0.0625
Outputs:
- layer_out: bfloat16 [2048, 16384], P('section', 'dp')
Inputs may be any that keep to these rules, and one draw needn't show every extreme that they name: A permutation that moves whole sentences: the rows of one sentence (a run of equal segments within a block of 32 rows) come from consecutive entry rows in order. `segments`: within each block of 32 rows the sentence numbers do not fall and each of 0 to 1 appears.
All inputs are finite; a program needn't handle non-finite values.
Results may differ from a plain program's by a relative error of at most 0.022.
Values may be sent and summed in bfloat16 or wider, within the bound.
No kernel may reach another device: no remote copies, remote signals or barrier semaphores. Data moves between devices by JAX's collectives and lax.ppermute only.
A program may use at most 64 MiB of HBM per device.

v0:
```python
import math
import jax
import jax.numpy as jnp
from jax import lax
from jax.experimental.layout import Layout, with_layout_constraint
from jax.sharding import PartitionSpec as P

MODEL_WIDTH = 16384
KEYVALUE_HEADS = 8
QUERY_HEADS = 64
MICRO_TOKENS = 32
HEAD_WIDTH = 128
SPARE_COLUMNS = 128
M = 4
norm_epsilon = 1e-05


def causal_block_attend(query_rows, key_value_rows, allowed, query_group_width):
    block_count, row_count = allowed.shape[:2]
    kv_heads = key_value_rows.shape[1]
    head_size = key_value_rows.shape[2] // 2
    query_head_rows = query_rows.reshape(
        block_count, row_count, kv_heads, query_group_width, head_size
    )
    key_value_blocks = key_value_rows.reshape(block_count, row_count, kv_heads, 2 * head_size)
    key_heads = key_value_blocks[..., :head_size]
    value_heads = key_value_blocks[..., head_size:]
    scores = jnp.einsum(
        "bqkgd,bskd->bkgqs", query_head_rows, key_heads, preferred_element_type=jnp.float32
    ) / math.sqrt(head_size)
    raw_weights = jnp.where(allowed[:, None, None], jnp.exp(scores), 0.0)
    totals = jnp.sum(raw_weights, axis=-1, keepdims=True)
    probs = (raw_weights / totals).astype(jnp.bfloat16)
    attended_rows = jnp.einsum(
        "bkgqs,bskd->bqkgd", probs, value_heads, preferred_element_type=jnp.float32
    )
    return attended_rows.astype(jnp.bfloat16).reshape(
        block_count * row_count, kv_heads * query_group_width * head_size
    )


def block_mask(sentence_segment_rows):
    row_count = sentence_segment_rows.shape[1]
    position = jnp.arange(row_count)
    return (sentence_segment_rows[:, :, None] == sentence_segment_rows[:, None, :]) & (
        position[None, :] <= position[:, None]
    )[None]


def gathered_over(block, axis):
    count = lax.axis_size(axis)
    spread = jnp.broadcast_to(block[None], (count,) + block.shape)
    return lax.all_to_all(spread, axis, 0, 0, tiled=False).reshape(
        (count * block.shape[0],) + block.shape[1:]
    )


def section_layer(hidden, own_allowed, gain_row, joined_weight, out_weight):
    row_count = hidden.shape[0]
    group_count = lax.axis_size("dp")
    own_rows = row_count // group_count
    widened = hidden.astype(jnp.float32)
    normed_rows = (widened * gain_row[None, :]).astype(jnp.bfloat16)
    joined_terms = jnp.dot(normed_rows, joined_weight, preferred_element_type=jnp.float32)
    query_width = out_weight.shape[0]
    keyval_width = joined_terms.shape[1] - query_width - SPARE_COLUMNS
    square_terms = jnp.sum(widened * widened, axis=1, keepdims=True)
    square_high = lax.reduce_precision(square_terms, exponent_bits=8, mantissa_bits=7)
    square_low = square_terms - square_high
    column = lax.broadcasted_iota(jnp.int32, joined_terms.shape, 1)
    square_column = query_width + keyval_width
    payload = jnp.where(
        column == square_column,
        square_high,
        jnp.where(column == square_column + 1, square_low, joined_terms),
    ).astype(jnp.bfloat16)
    arrived = lax.all_to_all(
        payload.reshape(group_count, own_rows, payload.shape[1]), "dp", 0, 0, tiled=False
    )
    summed = jnp.sum(arrived.astype(jnp.float32), axis=0)
    own_squares = summed[:, query_width + keyval_width] + summed[:, query_width + keyval_width + 1]
    root_mean_square = jnp.sqrt(own_squares / MODEL_WIDTH + norm_epsilon)
    scaled_sums = summed[:, : query_width + keyval_width] / root_mean_square[:, None]
    query_rows = scaled_sums[:, :query_width].astype(jnp.bfloat16)
    key_value_rows = (
        scaled_sums[:, query_width:].astype(jnp.bfloat16).reshape(own_rows, -1, 2 * HEAD_WIDTH)
    )
    attended_rows = causal_block_attend(
        query_rows, key_value_rows, own_allowed, QUERY_HEADS // KEYVALUE_HEADS
    )
    head_terms = jnp.dot(
        gathered_over(attended_rows, "dp"), out_weight, preferred_element_type=jnp.float32
    )
    head_total = lax.psum(head_terms.astype(jnp.bfloat16), "tensor").astype(jnp.float32)
    return (widened + head_total).astype(jnp.bfloat16)


def on_device(tokens, order, segments, gain, w_query, key_value_weight, w_out):
    section_count = lax.axis_size("section")
    section_index = lax.axis_index("section")
    group_count = lax.axis_size("dp")
    slice_width = w_query.shape[1]
    joined = jnp.concatenate(
        [
            w_query[0],
            key_value_weight[0].reshape(slice_width, -1),
            jnp.zeros((slice_width, SPARE_COLUMNS), w_query.dtype),
        ],
        axis=1,
    )
    own = (gain[0], joined, w_out[0])
    swap = [(i, (i + 1) % section_count) for i in range(section_count)]
    other = lax.ppermute(own, "section", swap)
    entry_rows, model_width = tokens.shape
    part_rows = entry_rows // section_count
    my_rows = lax.dynamic_slice_in_dim(tokens, section_index * part_rows, part_rows)
    got = lax.all_to_all(
        my_rows.reshape(part_rows, group_count, model_width // group_count), "dp", 1, 0, tiled=True
    ).reshape(group_count * part_rows, -1)
    received = lax.ppermute(got, "section", swap)
    rows_here = group_count * entry_rows // section_count
    own_blocks = rows_here // (group_count * MICRO_TOKENS)
    own_segments = lax.dynamic_slice_in_dim(
        segments,
        section_index * rows_here + lax.axis_index("dp") * own_blocks * MICRO_TOKENS,
        own_blocks * MICRO_TOKENS,
    ).reshape(own_blocks, MICRO_TOKENS)
    other, received, own_allowed = lax.optimization_barrier(
        (other, received, block_mask(own_segments))
    )
    my_order = lax.dynamic_slice_in_dim(order, section_index * rows_here, rows_here)
    source_group = my_order // entry_rows
    within = my_order % entry_rows
    from_other = within // part_rows != section_index
    block_index = source_group * part_rows + within % part_rows
    hits = lax.broadcasted_iota(jnp.int32, (rows_here, got.shape[0]), 1) == block_index[:, None]
    picked_here = (hits & ~from_other[:, None]).astype(got.dtype)
    picked_there = (hits & from_other[:, None]).astype(got.dtype)
    hidden = (
        jnp.dot(picked_here, got, preferred_element_type=jnp.float32)
        + jnp.dot(picked_there, received, preferred_element_type=jnp.float32)
    ).astype(got.dtype)
    hidden = with_layout_constraint(hidden, Layout(major_to_minor=(0, 1)))
    for layer_index in range(section_count):
        params = jax.tree.map(
            lambda mine, theirs: jnp.where(section_index == layer_index, mine, theirs), own, other
        )
        hidden = section_layer(hidden, own_allowed, *params)
    return hidden


def solution(mesh):
    placed = (
        P("dp", None),
        P(),
        P(),
        P("section", "dp"),
        P("section", "dp", "tensor"),
        P("section", "dp", "tensor", None),
        P("section", "tensor", "dp"),
    )
    return jax.shard_map(
        on_device, mesh=mesh, in_specs=placed, out_specs=P("section", "dp"), check_vma=False
    )
```

profile of v0, /device:TPU:2, one launch (start us, length us, event | category | flops | bytes accessed | tf_op | source)
XLA Modules:
  0.0 392.8 jit_solution(6139880613853147727)
XLA Ops:
  6.5 1.7 constant_dynamic-slice_fusion
  8.3 1.6 copy.54
  9.8 7.7 %all-to-all-start = ((bf16[64,16,1024]{2,0,1:T(8,128)(2,1)}), bf16[64,16,1024]{2,0,1:T(8,128)(2,1)}, u32[]{:S(2)}, u32[]{:S(2)}) async-start(bf16[64,16,1024]{2,0,1:T(8,128)(2,1)} %bitcast.102), calls=%async_computation | async-start | bytes 4194304 | tf_op jit(solution)/shard_map/all_to_all | solution.py:117
  17.6 0.0 copy-start.5
  17.6 0.0 all-reduce.3.cloned.1.call-start
  17.7 2.2 maximum_maximum_fusion
  19.9 0.5 collective-permute-start.2
  20.4 24.4 %all-to-all-done = bf16[64,16,1024]{2,0,1:T(8,128)(2,1)} async-done(((bf16[64,16,1024]{2,0,1:T(8,128)(2,1)}), bf16[64,16,1024]{2,0,1:T(8,128)(2,1)}, u32[]{:S(2)}, u32[]{:S(2)}) %all-to-all-start) | async-done | bytes 2097184 | tf_op jit(solution)/shard_map/all_to_all | solution.py:117
  44.8 0.0 collective-permute-start.3
  44.8 0.5 collective-permute-start
  45.3 0.8 dynamic_slice.11
  46.1 0.1 eq.52
  46.2 0.1 compare_and_fusion
  46.3 4.0 %fusion.8 = f32[1024,1024]{1,0:T(8,128)S(1)} fusion(bf16[1024,1024]{1,0:T(8,128)(2,1)} %bitcast.2, s32[1024]{0:T(1024)S(1)} %fusion.61, pred[1024]{0:T(1024)(128)(4,1)S(1)} %get-tuple-element.15), kind=kOutput, calls=%fused_computation.20 | convolution fusion | flops 2149580800 | bytes 6296576 | tf_op jit(solution)/shard_map/dot_general | solution.py:140
  50.3 0.0 collective-permute-done
  50.3 0.0 collective-permute-done.1
  50.3 0.0 copy-start.2
  50.4 4.9 %fusion = (f32[1024]{0:T(1024)S(1)}, bf16[1024,1024]{1,0:T(8,128)(2,1)S(1)}) fusion(f32[1024,1024]{1,0:T(8,128)S(1)} %fusion.8, bf16[1024,1024]{1,0:T(8,128)(2,1)} %collective-permute-done.3, s32[1024]{0:T(1024)S(1)} %fusion.61, pred[1024]{0:T(1024)(128)(4,1)S(1)} %get-tuple-element.16), kind=kOutput, calls=%fused_computation.10 | convolution fusion | flops 2154822656 | bytes 8397824 | tf_op jit(solution)/shard_map/dot_general | solution.py:141
  55.3 3.6 select_convert_fusion.1
  58.9 44.4 %all_to_all.35 = bf16[16,64,1408]{2,1,0:T(8,128)(2,1)S(1)} all-to-all(bf16[16,64,1408]{2,1,0:T(8,128)(2,1)S(1)} %bitcast.107), channel_id=1, replica_groups=mesh['dp'=16,'section'=2,'tensor'=8] {'dp'}, dimensions={0} | all-to-all | bytes 5767168 | tf_op jit(solution)/shard_map/all_to_all | solution.py:77
  103.3 0.4 convert_reduce_fusion.1
  103.6 0.2 fusion.59
  103.8 0.1 fusion.47
  104.0 0.3 fusion.73
  104.3 0.2 fusion.44
  104.6 0.1 copy.28
  104.7 0.3 broadcast_in_dim.78
  104.9 32.2 %all_to_all.36 = bf16[16,64,1024]{2,1,0:T(8,128)(2,1)S(1)} all-to-all(bf16[16,64,1024]{2,1,0:T(8,128)(2,1)S(1)} %broadcast_in_dim.78), channel_id=1, replica_groups=mesh['dp'=16,'section'=2,'tensor'=8] {'dp'}, dimensions={0} | all-to-all | bytes 4194304 | tf_op jit(solution)/shard_map/all_to_all | solution.py:53
  137.1 5.3 %fusion.30 = bf16[1024,1024]{1,0:T(8,128)(2,1)} fusion(bf16[1024,1024]{1,0:T(8,128)(2,1)S(1)} %bitcast.112, bf16[1024,1024]{1,0:T(8,128)(2,1)} %collective-permute-done.2, pred[]{:T(512)S(6)} %eq.58, bf16[1,1024,1024]{2,1,0:T(8,128)(2,1)} %param.13), kind=kOutput, calls=%fused_computation.40 | convolution fusion | flops 2149580800 | bytes 8388609 | tf_op jit(solution)/shard_map/dot_general | solution.py:91
  142.4 0.0 all-reduce.3.cloned.1.call-update
  142.4 0.0 all-reduce.5.cloned.1.call-start
  142.4 82.2 %all-reduce.3.cloned.1.call-done = bf16[1024,1024]{1,0:T(8,128)(2,1)} async-done(((bf16[1024,1024]{1,0:T(8,128)(2,1)}), bf16[1024,1024]{1,0:T(8,128)(2,1)}) %all-reduce.3.cloned.1.call-update) | async-done | bytes 2097168 | tf_op jit(solution)/shard_map/psum | solution.py:94
  224.6 2.5 fusion.3
  227.1 0.3 copy-done.3
  227.5 5.4 %select_convert_fusion = bf16[1024,1408]{1,0:T(8,128)(2,1)S(1)} fusion(bf16[1024,1408]{1,0:T(8,128)(2,1)} %collective-permute-done.1, bf16[1024]{0:T(1024)(128)(2,1)S(1)} %get-tuple-element.20, bf16[1024]{0:T(1024)(128)(2,1)S(1)} %get-tuple-element.19, pred[]{:T(512)S(6)} %eq.59, pred[1408]{0:T(1024)(128)(4,1)S(1)} %get-tuple-element.29, ...), kind=kOutput, calls=%fused_computation.7 | convolution fusion | flops 2973106176 | bytes 12596737 | tf_op jit(solution)/shard_map/dot_general | solution.py:64
  232.9 37.0 %all_to_all.37 = bf16[16,64,1408]{2,1,0:T(8,128)(2,1)S(1)} all-to-all(bf16[16,64,1408]{2,1,0:T(8,128)(2,1)S(1)} %bitcast.106), channel_id=1, replica_groups=mesh['dp'=16,'section'=2,'tensor'=8] {'dp'}, dimensions={0} | all-to-all | bytes 5767168 | tf_op jit(solution)/shard_map/all_to_all | solution.py:77
  269.8 0.4 convert_reduce_fusion
  270.2 0.2 fusion.55
  270.4 0.1 fusion.46
  270.6 0.3 fusion.74
  270.9 0.2 fusion.45
  271.2 0.1 copy.31
  271.2 0.3 broadcast_in_dim.82
  271.5 25.5 %all_to_all.38 = bf16[16,64,1024]{2,1,0:T(8,128)(2,1)S(1)} all-to-all(bf16[16,64,1024]{2,1,0:T(8,128)(2,1)S(1)} %broadcast_in_dim.82), channel_id=1, replica_groups=mesh['dp'=16,'section'=2,'tensor'=8] {'dp'}, dimensions={0} | all-to-all | bytes 4194304 | tf_op jit(solution)/shard_map/all_to_all | solution.py:53
  297.0 5.9 %fusion.33 = bf16[1024,1024]{1,0:T(8,128)(2,1)} fusion(bf16[1024,1024]{1,0:T(8,128)(2,1)S(1)} %bitcast.111, bf16[1024,1024]{1,0:T(8,128)(2,1)} %collective-permute-done.2, pred[]{:T(512)S(6)} %eq.59, bf16[1,1024,1024]{2,1,0:T(8,128)(2,1)} %param.13), kind=kOutput, calls=%fused_computation.41 | convolution fusion | flops 2149580800 | bytes 8388609 | tf_op jit(solution)/shard_map/dot_general | solution.py:91
  302.9 0.0 all-reduce.5.cloned.1.call-update
  302.9 78.0 %all-reduce.5.cloned.1.call-done = bf16[1024,1024]{1,0:T(8,128)(2,1)} async-done(((bf16[1024,1024]{1,0:T(8,128)(2,1)}), bf16[1024,1024]{1,0:T(8,128)(2,1)}) %all-reduce.5.cloned.1.call-update) | async-done | bytes 2097168 | tf_op jit(solution)/shard_map/psum | solution.py:94
  380.9 5.0 %fusion.5 = bf16[1024,1024]{1,0:T(8,128)(2,1)} fusion(bf16[1024,1024]{1,0:T(8,128)(2,1)} %all-reduce.5.cloned.1.call-done, bf16[1024,1024]{1,0:T(8,128)(2,1)} %all-reduce.3.cloned.1.call-done, bf16[1024,1024]{1,0:T(8,128)(2,1)S(1)} %get-tuple-element.24), kind=kLoop, calls=%fused_computation.15 | loop fusion | flops 8388608 | bytes 8388608 | tf_op jit(solution)/shard_map/convert_element_type | solution.py:95
  (31 shorter events, 0.2 us)
Async XLA Ops:
  9.8 7.8 %copy-start.1 = (bf16[1,1024,1024]{2,1,0:T(8,128)(2,1)S(1)}, bf16[1,1024,1024]{2,1,0:T(8,128)(2,1)}, u32[]{:S(2)}) copy-start(bf16[1,1024,1024]{2,1,0:T(8,128)(2,1)} %param.11) | copy-start | bytes 6291460
  9.8 7.8 %copy-start.4 = (bf16[1,1024,1,256]{3,1,2,0:T(8,128)(2,1)S(1)}, bf16[1,1024,1,256]{3,1,2,0:T(8,128)(2,1)}, u32[]{:S(2)}) copy-start(bf16[1,1024,1,256]{3,1,2,0:T(8,128)(2,1)} %param.12) | copy-start | bytes 1572868
  9.8 35.0 %all-to-all-start = ((bf16[64,16,1024]{2,0,1:T(8,128)(2,1)}), bf16[64,16,1024]{2,0,1:T(8,128)(2,1)}, u32[]{:S(2)}, u32[]{:S(2)}) async-start(bf16[64,16,1024]{2,0,1:T(8,128)(2,1)} %bitcast.102), calls=%async_computation | async-start | bytes 4194304 | tf_op jit(solution)/shard_map/all_to_all | solution.py:117
  17.6 27.2 %copy-start.6 = (f32[1,1024]{1,0:T(1,128)S(1)}, f32[1,1024]{1,0:T(1,128)}, u32[]{:S(2)}) copy-start(f32[1,1024]{1,0:T(1,128)} %param.10) | copy-start | bytes 12292
  17.6 28.6 %copy-start.5 = (s32[2048]{0:T(1024)S(1)}, s32[2048]{0:T(1024)}, u32[]{:S(2)}) copy-start(s32[2048]{0:T(1024)} %param.8) | copy-start | bytes 24580
  17.6 207.0 %all-reduce.3.cloned.1.call-start = ((), (), s32[]{:S(2)}) async-start(), calls=%async_computation.5 | async-start | bytes 4194304 | tf_op jit(solution)/shard_map/psum | solution.py:94
  19.9 30.4 %collective-permute-start.1 = (bf16[1024,1408]{1,0:T(8,128)(2,1)}, bf16[1024,1408]{1,0:T(8,128)(2,1)}, u32[]{:S(2)}, u32[]{:S(2)}) collective-permute-start(bf16[1024,1408]{1,0:T(8,128)(2,1)} %maximum_maximum_fusion), channel_id=1, source_target_pairs={{0,8},{8,0},{1,9},{9,1},{2,10},{10,2},{3,11},{11,3},{4,12},{12,4},... | collective-permute-start | bytes 8650760 | tf_op jit(solution)/shard_map/ppermute | solution.py:113
  19.9 30.4 %collective-permute-start.2 = (bf16[1024,1024]{1,0:T(8,128)(2,1)}, bf16[1024,1024]{1,0:T(8,128)(2,1)}, u32[]{:S(2)}, u32[]{:S(2)}) collective-permute-start(bf16[1024,1024]{1,0:T(8,128)(2,1)} %bitcast.6), channel_id=1, source_target_pairs={{0,8},{8,0},{1,9},{9,1},{2,10},{10,2},{3,11},{11,3},{4,12},{12,4},... | collective-permute-start | bytes 6291464 | tf_op jit(solution)/shard_map/ppermute | solution.py:113
  44.8 5.5 %collective-permute-start.3 = (bf16[1024,1024]{1,0:T(8,128)(2,1)}, bf16[1024,1024]{1,0:T(8,128)(2,1)}, u32[]{:S(2)}, u32[]{:S(2)}) collective-permute-start(bf16[1024,1024]{1,0:T(8,128)(2,1)} %bitcast.2), channel_id=1, source_target_pairs={{0,8},{8,0},{1,9},{9,1},{2,10},{10,2},{3,11},{11,3},{4,12},{12,4},... | collective-permute-start | bytes 6291464 | tf_op jit(solution)/shard_map/ppermute | solution.py:120
  44.8 5.5 %collective-permute-start = (f32[1024]{0:T(1024)S(1)}, f32[1024]{0:T(1024)S(1)}, u32[]{:S(2)}, u32[]{:S(2)}) collective-permute-start(f32[1024]{0:T(1024)S(1)} %bitcast.126), channel_id=1, source_target_pairs={{0,8},{8,0},{1,9},{9,1},{2,10},{10,2},{3,11},{11,3},{4,12},{12,4},... | collective-permute-start | bytes 12296 | tf_op jit(solution)/shard_map/ppermute | solution.py:113
  50.3 4.9 %copy-start.2 = (bf16[1,1024,1024]{2,1,0:T(8,128)(2,1)S(1)}, bf16[1,1024,1024]{2,1,0:T(8,128)(2,1)}, u32[]{:S(2)}) copy-start(bf16[1,1024,1024]{2,1,0:T(8,128)(2,1)} %param.11) | copy-start | bytes 6291460
  142.4 238.5 %all-reduce.5.cloned.1.call-start = ((), (), s32[]{:S(2)}) async-start(), calls=%async_computation.6 | async-start | bytes 4194304 | tf_op jit(solution)/shard_map/psum | solution.py:94
  224.6 2.5 copy-start
  224.6 2.9 copy-start.3
Sparse Core Ops, SparseCore 0:
  142.5 82.0 all-reduce.2
  303.1 77.8 all-reduce.4
where the time goes:
time: 393 us
  waiting for transfers between devices  185 us (47%)
  blocking collectives  139 us (35%)
  matrix products  30.1 us (8%)
  between operations  13.7 us (3%)
  other arithmetic  11.2 us (3%)
  starting transfers between devices  8.84 us (2%)
  local copies, waits for them, and re-layouts  5.23 us (1%)
    psum x2, waiting for transfers between devices, section_layer(): lax.psum(head_terms.astype(jnp.bfloat16), 'tensor').astype(jnp.float32)  160 us
    all_to_all x2, blocking collectives, section_layer(): lax.all_to_all(payload.reshape(group_count, own_rows, payload.shape[1]),...  81.4 us
    all_to_all x2, blocking collectives, gathered_over(): lax.all_to_all(spread, axis, 0, 0, tiled=False)  57.7 us
    all_to_all x1, waiting for transfers between devices, on_device(): lax.all_to_all(my_rows.reshape(part_rows, group_count, model_width // gro...  24.4 us
    dot_general x2, matrix products, section_layer(): jnp.dot(gathered_over(attended_rows, 'dp'), out_weight, preferred_element...  11.2 us
    dot_general x2, matrix products, section_layer(): jnp.dot(normed_rows, joined_weight, preferred_element_type=jnp.float32)  8.97 us
  transfers between devices with their start and end apart: 7, of which 3 were waited for; matrix products, arithmetic and copies ran while one was open for 2% of the time, Pallas kernels for 0%

commit v1 on v0

--- a/solution.py
+++ b/solution.py
@@ -13,6 +13,12 @@
 SPARE_COLUMNS = 128
 M = 4
 norm_epsilon = 1e-05
+
+
+def resolve_streams_over_axis(obj):
+    ready = lax.all_gather(obj, "tensor")
+    piece_out = jnp.sum(ready, 0)
+    return piece_out
 
 
 def causal_block_attend(query_rows, key_value_rows, allowed, query_group_width):
@@ -91,7 +97,7 @@
     head_terms = jnp.dot(
         gathered_over(attended_rows, "dp"), out_weight, preferred_element_type=jnp.float32
     )
-    head_total = lax.psum(head_terms.astype(jnp.bfloat16), "tensor").astype(jnp.float32)
+    head_total = resolve_streams_over_axis(head_terms.astype(jnp.bfloat16)).astype(jnp.float32)
     return (widened + head_total).astype(jnp.bfloat16)
 
 

time: 393 us -> 602 us (1.53)
  waiting for transfers between devices: 185 us -> 366 us
  other arithmetic: 11.2 us -> 31.5 us
  blocking collectives: 139 us -> 146 us
    all_gather x0 -> x2, waiting for transfers between devices: none -> 341 us  [resolve_streams_over_axis(): ready = lax.all_gather(obj, 'tensor')]
    psum x2 -> x0, waiting for transfers between devices: 160 us -> none  [section_layer(): lax.psum(head_terms.astype(jnp.bfloat16), 'tensor').astype(jnp.float32)]
    reduce_sum x0 -> x2, other arithmetic: none -> 20.2 us  [resolve_streams_over_axis(): piece_out = jnp.sum(ready, 0)]
  transfers between devices with their start and end apart: 7 -> 7, of which waited for: 3 -> 3; matrix products, arithmetic and copies ran while one was open for 2% -> 1% of each run, Pallas kernels for 0% -> 0%
where the time goes in v1:
time: 602 us; the launch traced here: 601 us
  waiting for transfers between devices  366 us (61%)
  blocking collectives  146 us (24%)
  other arithmetic  31.5 us (5%)
  matrix products  30.1 us (5%)
  between operations  13.8 us (2%)
  starting transfers between devices  8.79 us (1%)
    all_gather x2, waiting for transfers between devices, resolve_streams_over_axis(): ready = lax.all_gather(obj, 'tensor')  341 us
    all_to_all x2, blocking collectives, section_layer(): lax.all_to_all(payload.reshape(group_count, own_rows, payload.shape[1]),...  84.3 us
    all_to_all x2, blocking collectives, gathered_over(): lax.all_to_all(spread, axis, 0, 0, tiled=False)  61.4 us
    all_to_all x1, waiting for transfers between devices, on_device(): lax.all_to_all(my_rows.reshape(part_rows, group_count, model_width // gro...  24.3 us
    reduce_sum x2, other arithmetic, resolve_streams_over_axis(): piece_out = jnp.sum(ready, 0)  20.2 us
  transfers between devices with their start and end apart: 7, of which 3 were waited for; matrix products, arithmetic and copies ran while one was open for 1% of the time, Pallas kernels for 0%

profile of v1, /device:TPU:2, one launch (start us, length us, event | category | flops | bytes accessed | tf_op | source)
XLA Modules:
  0.0 600.8 jit_solution(11916533676684049530)
XLA Ops:
  6.5 1.7 constant_dynamic-slice_fusion
  8.3 1.5 copy.54
  9.8 7.6 %all-to-all-start = ((bf16[64,16,1024]{2,0,1:T(8,128)(2,1)}), bf16[64,16,1024]{2,0,1:T(8,128)(2,1)}, u32[]{:S(2)}, u32[]{:S(2)}) async-start(bf16[64,16,1024]{2,0,1:T(8,128)(2,1)} %bitcast.104), calls=%async_computation | async-start | bytes 4194304 | tf_op jit(solution)/shard_map/all_to_all | solution.py:123
  17.4 0.0 copy-start.5
  17.4 0.0 all-gather.5.cloned.1.call-start
  17.5 2.2 maximum_maximum_fusion
  19.7 0.1 collective-permute-start.1
  19.8 0.5 collective-permute-start.2
  20.3 24.3 %all-to-all-done = bf16[64,16,1024]{2,0,1:T(8,128)(2,1)} async-done(((bf16[64,16,1024]{2,0,1:T(8,128)(2,1)}), bf16[64,16,1024]{2,0,1:T(8,128)(2,1)}, u32[]{:S(2)}, u32[]{:S(2)}) %all-to-all-start) | async-done | bytes 2097184 | tf_op jit(solution)/shard_map/all_to_all | solution.py:123
  44.6 0.5 collective-permute-start
  45.1 0.8 dynamic_slice.11
  45.9 0.1 eq.52
  46.0 0.1 compare_and_fusion
  46.1 4.0 fusion.8
  50.2 4.9 fusion
  55.1 3.5 select_convert_fusion.1
  58.6 43.6 %all_to_all.35 = bf16[16,64,1408]{2,1,0:T(8,128)(2,1)S(1)} all-to-all(bf16[16,64,1408]{2,1,0:T(8,128)(2,1)S(1)} %bitcast.111), channel_id=1, replica_groups=mesh['dp'=16,'section'=2,'tensor'=8] {'dp'}, dimensions={0} | all-to-all | bytes 5767168 | tf_op jit(solution)/shard_map/all_to_all | solution.py:83
  102.3 0.4 convert_reduce_fusion.1
  102.7 0.2 fusion.59
  102.8 0.1 fusion.47
  103.0 0.3 fusion.73
  103.3 0.2 fusion.44
  103.6 0.1 copy.28
  103.7 0.3 broadcast_in_dim.78
  103.9 32.8 %all_to_all.36 = bf16[16,64,1024]{2,1,0:T(8,128)(2,1)S(1)} all-to-all(bf16[16,64,1024]{2,1,0:T(8,128)(2,1)S(1)} %broadcast_in_dim.78), channel_id=1, replica_groups=mesh['dp'=16,'section'=2,'tensor'=8] {'dp'}, dimensions={0} | all-to-all | bytes 4194304 | tf_op jit(solution)/shard_map/all_to_all | solution.py:59
  136.7 5.3 fusion.30
  142.0 0.0 all-gather.5.cloned.1.call-update
  142.0 0.0 all-gather.7.cloned.1.call-start
  142.1 172.8 %all-gather.5.cloned.1.call-done = bf16[8192,1024]{1,0:T(8,128)(2,1)} async-done(((bf16[1024,1024]{1,0:T(8,128)(2,1)}), bf16[8192,1024]{1,0:T(8,128)(2,1)}) %all-gather.5.cloned.1.call-update) | async-done | bytes 16777232 | tf_op jit(solution)/shard_map/all_gather | solution.py:19
  314.8 9.5 %reduce_sum.81 = bf16[1024,1024]{1,0:T(8,128)(2,1)S(1)} reduce(bf16[8,1024,1024]{2,1,0:T(8,128)(2,1)} %bitcast.107, bf16[]{:T(256)} %constant.80.clone.1), dimensions={0}, to_apply=%region_3.4 | reduce | flops 7340032 | bytes 18874370 | tf_op jit(solution)/shard_map/reduce_sum | solution.py:20
  324.3 0.0 copy-start.3
  324.3 2.5 fusion.3
  326.8 0.3 copy-done.3
  327.2 5.4 select_convert_fusion
  332.6 40.7 %all_to_all.37 = bf16[16,64,1408]{2,1,0:T(8,128)(2,1)S(1)} all-to-all(bf16[16,64,1408]{2,1,0:T(8,128)(2,1)S(1)} %bitcast.110), channel_id=1, replica_groups=mesh['dp'=16,'section'=2,'tensor'=8] {'dp'}, dimensions={0} | all-to-all | bytes 5767168 | tf_op jit(solution)/shard_map/all_to_all | solution.py:83
  373.3 0.4 convert_reduce_fusion
  373.7 0.2 fusion.55
  373.9 0.1 fusion.46
  374.0 0.3 fusion.74
  374.4 0.2 fusion.45
  374.6 0.1 copy.31
  374.7 0.3 broadcast_in_dim.82
  375.0 28.6 %all_to_all.38 = bf16[16,64,1024]{2,1,0:T(8,128)(2,1)S(1)} all-to-all(bf16[16,64,1024]{2,1,0:T(8,128)(2,1)S(1)} %broadcast_in_dim.82), channel_id=1, replica_groups=mesh['dp'=16,'section'=2,'tensor'=8] {'dp'}, dimensions={0} | all-to-all | bytes 4194304 | tf_op jit(solution)/shard_map/all_to_all | solution.py:59
  403.6 5.9 fusion.33
  409.5 0.0 all-gather.7.cloned.1.call-update
  409.5 168.6 %all-gather.7.cloned.1.call-done = bf16[8192,1024]{1,0:T(8,128)(2,1)} async-done(((bf16[1024,1024]{1,0:T(8,128)(2,1)}), bf16[8192,1024]{1,0:T(8,128)(2,1)}) %all-gather.7.cloned.1.call-update) | async-done | bytes 16777232 | tf_op jit(solution)/shard_map/all_gather | solution.py:19
  578.2 10.8 %reduce_sum.85 = bf16[1024,1024]{1,0:T(8,128)(2,1)} reduce(bf16[8,1024,1024]{2,1,0:T(8,128)(2,1)} %bitcast.108, bf16[]{:T(256)} %constant.80.clone.1), dimensions={0}, to_apply=%region_7.8 | reduce | flops 7340032 | bytes 18874370 | tf_op jit(solution)/shard_map/reduce_sum | solution.py:20
  588.9 5.0 fusion.5
  (33 shorter events, 0.2 us)
Async XLA Ops:
  9.8 7.7 %copy-start.4 = (bf16[1,1024,1,256]{3,1,2,0:T(8,128)(2,1)S(1)}, bf16[1,1024,1,256]{3,1,2,0:T(8,128)(2,1)}, u32[]{:S(2)}) copy-start(bf16[1,1024,1,256]{3,1,2,0:T(8,128)(2,1)} %param.12) | copy-start | bytes 1572868
  9.8 34.8 %all-to-all-start = ((bf16[64,16,1024]{2,0,1:T(8,128)(2,1)}), bf16[64,16,1024]{2,0,1:T(8,128)(2,1)}, u32[]{:S(2)}, u32[]{:S(2)}) async-start(bf16[64,16,1024]{2,0,1:T(8,128)(2,1)} %bitcast.104), calls=%async_computation | async-start | bytes 4194304 | tf_op jit(solution)/shard_map/all_to_all | solution.py:123
  17.4 27.2 %copy-start.6 = (f32[1,1024]{1,0:T(1,128)S(1)}, f32[1,1024]{1,0:T(1,128)}, u32[]{:S(2)}) copy-start(f32[1,1024]{1,0:T(1,128)} %param.10) | copy-start | bytes 12292
  17.4 28.6 %copy-start.5 = (s32[2048]{0:T(1024)S(1)}, s32[2048]{0:T(1024)}, u32[]{:S(2)}) copy-start(s32[2048]{0:T(1024)} %param.8) | copy-start | bytes 24580
  17.4 297.4 %all-gather.5.cloned.1.call-start = ((), (), s32[]{:S(2)}) async-start(), calls=%async_computation.5 | async-start | bytes 18874368 | tf_op jit(solution)/shard_map/all_gather | solution.py:19
  19.7 30.4 %collective-permute-start.1 = (bf16[1024,1408]{1,0:T(8,128)(2,1)S(1)}, bf16[1024,1408]{1,0:T(8,128)(2,1)}, u32[]{:S(2)}, u32[]{:S(2)}) collective-permute-start(bf16[1024,1408]{1,0:T(8,128)(2,1)S(1)} %maximum_maximum_fusion), channel_id=1, source_target_pairs={{0,8},{8,0},{1,9},{9,1},{2,10},{10,2},{3,11},{11,3},{4,12},{12,4},... | collective-permute-start | bytes 8650760 | tf_op jit(solution)/shard_map/ppermute | solution.py:119
  19.8 30.3 %collective-permute-start.2 = (bf16[1024,1024]{1,0:T(8,128)(2,1)}, bf16[1024,1024]{1,0:T(8,128)(2,1)}, u32[]{:S(2)}, u32[]{:S(2)}) collective-permute-start(bf16[1024,1024]{1,0:T(8,128)(2,1)} %bitcast.6), channel_id=1, source_target_pairs={{0,8},{8,0},{1,9},{9,1},{2,10},{10,2},{3,11},{11,3},{4,12},{12,4},... | collective-permute-start | bytes 6291464 | tf_op jit(solution)/shard_map/ppermute | solution.py:119
  44.6 5.5 collective-permute-start.3
  44.6 5.5 collective-permute-start
  50.1 4.9 copy-start.2
  55.0 3.6 copy-start
  142.0 436.1 %all-gather.7.cloned.1.call-start = ((), (), s32[]{:S(2)}) async-start(), calls=%async_computation.6 | async-start | bytes 18874368 | tf_op jit(solution)/shard_map/all_gather | solution.py:19
  324.3 2.5 copy-start.1
  324.3 2.8 copy-start.3
Sparse Core Ops, SparseCore 0:
  142.1 172.6 all-gather.4
  409.6 168.4 all-gather.6
